TPU v7x, 32 devices: a whole 2x2x4 slice. The times are simulated.
32 devices in a mesh: cells: 8 (over z, y), slab: 4 (over x, core).
Axes of the slice: x: 2, y: 2, z: 4, core: 2. Of those that a mesh axis runs over, the one named last changes fastest.
Arguments:
- grad: float32 [2, 2, 64, 8192], P(None, None, 'slab', 'cells'), may hold values from -6 to 6
- acc_block: float32 [2, 4, 64, 8192], P(None, None, 'slab', 'cells')
- mobility: float32 [2, 2, 64, 8192], P(None, None, 'slab', 'cells'), may hold values from 0.2 to 1.5
- store: float32 [2, 2, 64, 8192], P(None, None, 'slab', 'cells'), may hold values from 0.1 to 0.5
- trans_h: float32 [64, 8192], P('slab', 'cells'), may hold values from 0.3 to 3
- trans_v: float32 [64, 8192], P('slab', 'cells'), may hold values from 0.3 to 3
- fault_near: int32 [4, 16384], P('slab', 'cells'), may hold values from 0 to 16383
- fault_far: int32 [4, 16384], P('slab', 'cells'), may hold values from 0 to 16383
- fault_trans: float32 [4, 16384], P('slab', 'cells'), may hold values from 0.3 to 3
- fault_count: int32 [4, 8], P('slab', 'cells'), may hold values from 256 to 2048, as said below
- compl_cell: int32 [4, 1024], P('slab', 'cells'), may hold values from 0 to 16383
- compl_well: int32 [4, 1024], P('slab', 'cells'), may hold values from 0 to 15, as said below
- compl_wi: float32 [4, 1024], P('slab', 'cells'), may hold values from 0.5 to 5
Outputs:
- adjoint: float32 [2, 2, 64, 8192], P(None, None, 'slab', 'cells')
- res_history: float32 [2, 2], replicated
Inputs may be any that keep to these rules, and one draw needn't show every extreme that they name: `fault_count`: slots past a pair's count are padding; in every draw some pair of column blocks c, c+1 with c < 7 holds exactly 2048 live slots; the count of the last column block is unused. `compl_well`: every well of a group has at least one completion on the group's device of slab 0.
All inputs are finite; a program needn't handle non-finite values.
Results may differ from a plain program's by a relative error of at most 0.0001.
Values sent between devices are 32-bit elements; how exact they have to be, the bound alone decides.
No kernel may reach another device: no remote copies, remote signals or barrier semaphores. Data moves between devices by JAX's collectives and lax.ppermute only.
A program may use at most 128 MiB of HBM per device.

v0:
```python
import jax
import jax.numpy as jnp
from jax import lax
from jax.sharding import PartitionSpec as P

WELLS = 16
NSTEPS = 2


def shifted(value, axis, by):
    length = lax.axis_size(axis)
    pairs = [(i, i + by) for i in range(length) if 0 <= i + by < length]
    return lax.ppermute(value, axis, pairs)


def extended(block, sides, width):
    for axis, dim in sides:
        count = lax.axis_size(axis)
        forward = [(i, i + 1) for i in range(count - 1)]
        backward = [(target, source) for source, target in forward]
        low = lax.ppermute(
            lax.slice_in_dim(block, block.shape[dim] - width, None, axis=dim), axis, forward
        )
        high = lax.ppermute(lax.slice_in_dim(block, 0, width, axis=dim), axis, backward)
        block = jnp.concatenate([low, block, high], axis=dim)
    return block


def squares(residual):
    return lax.psum(jnp.sum(residual * residual), ("cells", "slab"))


def per_device(
    grad,
    acc_block,
    mobility,
    store,
    trans_h,
    trans_v,
    fault_near,
    fault_far,
    fault_trans,
    fault_count,
    compl_cell,
    compl_well,
    compl_wi,
):
    highest = lax.Precision.HIGHEST
    layer_count, column_count = trans_h.shape
    cells_size = lax.axis_size("cells")
    slab_size = lax.axis_size("slab")
    cells_place = lax.axis_index("cells")
    slab_place = lax.axis_index("slab")
    column_ids = lax.broadcasted_iota(jnp.int32, (layer_count, column_count), 1)
    layer_ids = lax.broadcasted_iota(jnp.int32, (layer_count, column_count), 0)
    zero_value = jnp.zeros((), trans_h.dtype)
    trans_east = jnp.where(
        (cells_place == cells_size - 1) & (column_ids == column_count - 1), zero_value, trans_h
    )
    trans_down = jnp.where(
        (slab_place == slab_size - 1) & (layer_ids == layer_count - 1), zero_value, trans_v
    )
    east_edge = shifted(trans_east[:, -1], "cells", 1)
    down_edge = shifted(trans_down[-1, :], "slab", 1)
    trans_west = jnp.concatenate([east_edge[:, None], trans_east[:, :-1]], axis=1)
    trans_up = jnp.concatenate([down_edge[None, :], trans_down[:-1, :]], axis=0)
    face_total = trans_east + trans_west + trans_down + trans_up
    near_cells = fault_near.reshape(-1)
    far_cells = fault_far.reshape(-1)
    slot_count = near_cells.shape[0]
    slot_live = (jnp.arange(slot_count, dtype=jnp.int32) < fault_count.reshape(())) & (
        cells_place < cells_size - 1
    )
    weight_here = jnp.where(slot_live, fault_trans.reshape(-1), zero_value)
    weight_left = shifted(weight_here, "cells", 1)
    well_cells = compl_cell.reshape(-1)
    well_index = compl_wi.reshape(-1)
    well_onehot = (
        compl_well.reshape(-1)[:, None] == jnp.arange(WELLS, dtype=jnp.int32)[None, :]
    ).astype(trans_h.dtype)
    well_totals = lax.psum(jnp.dot(well_index, well_onehot, precision=highest), "slab")
    solutions = [None] * NSTEPS
    histories = [None] * NSTEPS
    adjoint_next = jnp.zeros(grad.shape[1:], grad.dtype)
    for newton in range(NSTEPS - 1, -1, -1):
        block = acc_block[newton]
        mobile = mobility[newton]
        diag_first = block[0] + mobile[0] * face_total
        diag_second = block[3] + mobile[1] * face_total
        determinant = diag_first * diag_second - block[1] * block[2]
        inverse_aa = diag_second / determinant
        inverse_ab = -block[1] / determinant
        inverse_ba = -block[2] / determinant
        inverse_bb = diag_first / determinant
        residual = grad[newton] + store[newton] * adjoint_next
        history = []
        norm_square = squares(residual)
        precond = jnp.stack(
            [
                inverse_aa * residual[0] + inverse_ab * residual[1],
                inverse_ba * residual[0] + inverse_bb * residual[1],
            ]
        )
        scaled = mobile * precond
        flat = scaled.reshape(2, -1)
        picks_near = flat[:, near_cells]
        picks_far = flat[:, far_cells]
        padded = extended(scaled, (("cells", 2), ("slab", 1)), 1)
        east = padded[:, 1:-1, 2:]
        west = padded[:, 1:-1, :-2]
        below = padded[:, 2:, 1:-1]
        above = padded[:, :-2, 1:-1]
        from_left = shifted(picks_near, "cells", 1)
        from_right = shifted(picks_far, "cells", -1)
        laplace = (
            trans_east * (scaled - east)
            + trans_west * (scaled - west)
            + trans_down * (scaled - below)
            + trans_up * (scaled - above)
        )
        flux_right = weight_here * (picks_near - from_right)
        flux_left = weight_left * (from_left - picks_far)
        fault_term = (
            jnp.zeros_like(flat).at[:, near_cells].add(flux_right).at[:, far_cells].add(-flux_left)
        )
        fault_term = fault_term.reshape(2, layer_count, column_count)
        pressure = precond[0].reshape(-1)
        values = pressure[well_cells]
        rates = lax.psum(jnp.dot(well_index * values, well_onehot, precision=highest), "slab")
        back = jnp.dot(well_onehot, rates / well_totals, precision=highest)
        well_term = (
            jnp.zeros_like(pressure)
            .at[well_cells]
            .add(well_index * (values - back))
            .reshape(layer_count, column_count)
        )
        first = (
            block[0] * precond[0] + block[1] * precond[1] + laplace[0] + fault_term[0] + well_term
        )
        second = block[2] * precond[0] + block[3] * precond[1] + laplace[1] + fault_term[1]
        image = jnp.stack([first, second])
        along, energy = lax.psum(
            (jnp.sum(residual * image), jnp.sum(image * image)), ("cells", "slab")
        )
        history.append(jnp.sqrt(norm_square))
        alpha = along / energy
        solution = alpha * precond
        residual = residual - alpha * image
        closing = squares(residual)
        history.append(jnp.sqrt(closing))
        solutions[newton] = solution
        histories[newton] = jnp.stack(history)
        adjoint_next = solution
    return (jnp.stack(solutions), jnp.stack(histories))


def solution(mesh):
    placed = (
        P(None, None, "slab", "cells"),
        P(None, None, "slab", "cells"),
        P(None, None, "slab", "cells"),
        P(None, None, "slab", "cells"),
        P("slab", "cells"),
        P("slab", "cells"),
        P("slab", "cells"),
        P("slab", "cells"),
        P("slab", "cells"),
        P("slab", "cells"),
        P("slab", "cells"),
        P("slab", "cells"),
        P("slab", "cells"),
    )
    return jax.shard_map(
        per_device,
        mesh=mesh,
        in_specs=placed,
        out_specs=(P(None, None, "slab", "cells"), P()),
        check_vma=False,
    )
```

profile of v0, /device:TPU:0, one launch (start us, length us, event | category | flops | bytes accessed | tf_op | source)
XLA Modules:
  0.0 379.6 jit_solution(11750703015133822277)
XLA Ops:
  0.6 0.9 broadcast_select_fusion.1
  1.7 4.9 %collective-permute-start = (f32[16]{0:T(128)S(1)}, f32[16]{0:T(128)S(1)}, u32[]{:S(2)}, u32[]{:S(2)}) collective-permute-start(f32[16]{0:T(128)S(1)} %slice_reduce_fusion.4), channel_id=1, source_target_pairs={{0,4},{4,8},{8,12},{12,16},{16,20},{20,24},{24,28},{1,5},{5,9},{9,... | collective-permute-start | bytes 200 | tf_op jit(solution)/shard_map/ppermute | solution.py:13
  6.6 0.9 broadcast_select_fusion
  7.5 1.5 collective-permute-start.1
  9.6 0.7 fusion.81
  10.3 3.4 collective-permute-start.7
  13.8 1.0 fusion.91
  14.7 0.7 compare_select_fusion
  15.5 0.7 compare_select_fusion.1
  16.2 0.7 and_select_fusion
  16.9 0.7 fusion.83
  17.6 1.0 multiply_add_fusion
  18.6 0.9 convolution_bitcast_fusion.3
  19.6 4.6 %copy.39 = f32[1,2,16,1024]{1,3,2,0:T(8,128)} copy(f32[1,2,16,1024]{3,2,1,0:T(8,128)S(1)} %get-tuple-element.35) | data formatting | bytes 262144 | tf_op jit(solution)/shard_map/slice | solution.py:87
  24.2 4.7 %copy.45 = f32[1,2,16,1024]{1,3,2,0:T(8,128)} copy(f32[1,2,16,1024]{3,2,1,0:T(8,128)S(1)} %get-tuple-element.34) | data formatting | bytes 262144 | tf_op jit(solution)/shard_map/slice | solution.py:87
  29.4 5.0 %copy.40 = f32[2,16384]{0,1:T(8,128)} copy(f32[2,16384]{1,0:T(2,128)S(1)} %pad_maximum_fusion.10) | data formatting | bytes 262144 | tf_op jit(solution)/shard_map/stack | solution.py:98
  34.4 9.8 %bitcast_multiply_fusion.1 = f32[2,16384]{0,1:T(8,128)} fusion(f32[2,16384]{0,1:T(8,128)} %copy.40, f32[1,2,16,1024]{1,3,2,0:T(8,128)} %copy.39), kind=kLoop, calls=%fused_computation.17 | loop fusion | flops 32768 | bytes 393216 | tf_op jit(solution)/shard_map/mul | solution.py:104
  44.2 8.8 %gather_fusion.1 = f32[2048,2]{1,0:T(8,128)S(1)} fusion(f32[2,16384]{0,1:T(8,128)} %bitcast_multiply_fusion.1, s32[2048]{0:T(1024)S(1)} %broadcast_clamp_fusion), kind=kCustom, calls=%fused_computation.1 | custom fusion | bytes 40960 | tf_op jit(solution)/shard_map/gather | solution.py:107
  53.4 1.3 collective-permute-start.6
  54.7 8.8 %gather_fusion = f32[2048,2]{1,0:T(8,128)S(1)} fusion(f32[2,16384]{0,1:T(8,128)} %bitcast_multiply_fusion.1, s32[2048]{0:T(1024)S(1)} %broadcast_clamp_fusion.1), kind=kCustom, calls=%fused_computation | custom fusion | bytes 40960 | tf_op jit(solution)/shard_map/gather | solution.py:106
  63.9 4.5 %collective-permute-start.8 = (f32[2,2048]{1,0:T(2,128)S(1)}, f32[2,2048]{1,0:T(2,128)S(1)}, u32[]{:S(2)}, u32[]{:S(2)}) collective-permute-start(f32[2,2048]{1,0:T(2,128)S(1)} %bitcast.381), channel_id=1, source_target_pairs={{0,4},{4,8},{8,12},{12,16},{16,20},{20,24},{24,28},{1,5},{5,9},{9,... | collective-permute-start | bytes 49160 | tf_op jit(solution)/shard_map/ppermute | solution.py:13
  68.5 1.3 collective-permute-start.2
  69.8 5.0 %collective-permute-start.3 = (f32[2,16,1]{2,1,0:T(8,128)S(1)}, f32[2,16,1]{2,1,0:T(8,128)S(1)}, u32[]{:S(2)}, u32[]{:S(2)}) collective-permute-start(f32[2,16,1]{2,1,0:T(8,128)S(1)} %get-tuple-element.43), channel_id=1, source_target_pairs={{0,4},{4,8},{8,12},{12,16},{16,20},{20,24},{24,28},{1,5},{5,9},{9,... | collective-permute-start | bytes 392 | tf_op jit(solution)/shard_map/ppermute | solution.py:21
  74.8 1.1 gather_fusion.2
  76.2 6.6 %all-reduce.3 = (f32[16]{0:T(128)S(1)}, f32[16]{0:T(128)S(1)}) all-reduce(f32[16]{0:T(128)S(1)} %convolution_bitcast_fusion.4, f32[16]{0:T(128)S(1)} %convolution_bitcast_fusion.3), channel_id=1, replica_groups=mesh['cells'=8,'slab'=4] {'slab'}, use_global_device_ids=true, to_apply=%region_2.3 | all-reduce | flops 32 | bytes 256 | tf_op jit(solution)/shard_map/psum | solution.py:129
  82.9 1.3 collective-permute-start.4
  84.2 3.0 collective-permute-start.5
  87.5 1.3 scatter_custom_fusion.2
  89.2 0.4 copy.43
  89.6 15.2 %scatter_custom_fusion = f32[2,16384]{0,1:T(8,128)} fusion(s32[2048]{0:T(1024)S(1)} %bitcast.386, f32[2048,2]{1,0:T(8,128)S(1)} %copy.43, f32[]{:T(128)} %constant.10.clone.1), kind=kCustom, calls=%fused_computation.20 | custom fusion | flops 4096 | bytes 131076 | tf_op jit(solution)/shard_map/scatter-add | solution.py:124
  104.8 0.4 copy.44
  105.1 16.9 %scatter_fusion = f32[2,16384]{0,1:T(8,128)} fusion(f32[2,16384]{0,1:T(8,128)} %scatter_custom_fusion, s32[2048]{0:T(1024)S(1)} %bitcast.376, f32[2048,2]{1,0:T(8,128)S(1)} %copy.44), kind=kCustom, calls=%fused_computation.7 | custom fusion | flops 4096 | bytes 57344 | tf_op jit(solution)/shard_map/scatter-add | solution.py:124
  122.0 12.5 %slice_reduce_fusion.3 = (f32[16384]{0:T(1024)S(1)}, f32[16384]{0:T(1024)S(1)}) fusion(f32[2,16384]{0,1:T(8,128)} %scatter_fusion), kind=kLoop, calls=%fused_computation.15 | loop fusion | bytes 262144 | tf_op jit(solution)/shard_map/slice | solution.py:138
  134.7 0.7 multiply_reduce_fusion.4
  135.3 42.9 %all-reduce.2 = (f32[]{:T(128)}, f32[]{:T(128)}) all-reduce(f32[]{:T(128)} %get-tuple-element.13, f32[]{:T(128)} %get-tuple-element.12), channel_id=1, replica_groups=mesh['cells'=8,'slab'=4] {'cells','slab'}, use_global_device_ids=true, to_apply=%region_6.7 | all-reduce | flops 2 | bytes 16 | tf_op jit(solution)/shard_map/psum | solution.py:142
  180.0 5.0 %copy.46 = f32[2,16384]{0,1:T(8,128)} copy(f32[2,16384]{1,0:T(2,128)S(1)} %pad_maximum_fusion.12) | data formatting | bytes 262144 | tf_op jit(solution)/shard_map/stack | solution.py:98
  185.0 9.8 %bitcast_multiply_fusion = f32[2,16384]{0,1:T(8,128)} fusion(f32[2,16384]{0,1:T(8,128)} %copy.46, f32[1,2,16,1024]{1,3,2,0:T(8,128)} %copy.45), kind=kLoop, calls=%fused_computation.16 | loop fusion | flops 32768 | bytes 393216 | tf_op jit(solution)/shard_map/mul | solution.py:104
  194.7 8.8 %gather_fusion.3 = f32[2048,2]{1,0:T(8,128)S(1)} fusion(f32[2,16384]{0,1:T(8,128)} %bitcast_multiply_fusion, s32[2048]{0:T(1024)S(1)} %copy-done.13), kind=kCustom, calls=%fused_computation.3 | custom fusion | bytes 40960 | tf_op jit(solution)/shard_map/gather | solution.py:106
  203.6 9.8 %gather_fusion.4 = f32[2048,2]{1,0:T(8,128)S(1)} fusion(f32[2,16384]{0,1:T(8,128)} %bitcast_multiply_fusion, s32[2048]{0:T(1024)} %copy-done.11), kind=kCustom, calls=%fused_computation.4 | custom fusion | bytes 40960 | tf_op jit(solution)/shard_map/gather | solution.py:107
  213.4 1.5 fusion.31
  215.0 4.4 %collective-permute-start.10 = (f32[2,16,1]{2,1,0:T(8,128)S(1)}, f32[2,16,1]{2,1,0:T(8,128)S(1)}, u32[]{:S(2)}, u32[]{:S(2)}) collective-permute-start(f32[2,16,1]{2,1,0:T(8,128)S(1)} %get-tuple-element.41), channel_id=1, source_target_pairs={{0,4},{4,8},{8,12},{12,16},{16,20},{20,24},{24,28},{1,5},{5,9},{9,... | collective-permute-start | bytes 392 | tf_op jit(solution)/shard_map/ppermute | solution.py:21
  219.4 1.3 collective-permute-start.9
  221.0 4.5 %collective-permute-start.14 = (f32[2,2048]{1,0:T(2,128)S(1)}, f32[2,2048]{1,0:T(2,128)S(1)}, u32[]{:S(2)}, u32[]{:S(2)}) collective-permute-start(f32[2,2048]{1,0:T(2,128)S(1)} %bitcast.382), channel_id=1, source_target_pairs={{0,4},{4,8},{8,12},{12,16},{16,20},{20,24},{24,28},{1,5},{5,9},{9,... | collective-permute-start | bytes 49160 | tf_op jit(solution)/shard_map/ppermute | solution.py:13
  225.9 1.3 collective-permute-start.13
  227.2 1.3 gather_fusion.5
  228.5 0.9 convolution_bitcast_fusion.1
  229.4 5.8 %psum.81 = f32[16]{0:T(128)S(1)} all-reduce(f32[16]{0:T(128)S(1)} %convolution_bitcast_fusion.1), channel_id=1, replica_groups=mesh['cells'=8,'slab'=4] {'slab'}, use_global_device_ids=true, to_apply=%region_11.12 | all-reduce | flops 16 | bytes 128 | tf_op jit(solution)/shard_map/psum | solution.py:129
  235.3 1.3 collective-permute-start.11
  236.6 3.0 collective-permute-start.12
  239.6 0.9 fusion.7
  240.5 1.5 scatter_custom_fusion.5
  242.0 1.8 fusion.10
  243.8 0.7 negate_bitcast_fusion
  244.5 0.4 copy.50
  245.0 0.4 copy.49
  245.3 15.3 %scatter_custom_fusion.3 = f32[2,16384]{0,1:T(8,128)} fusion(s32[2048]{0:T(1024)} %bitcast.387, f32[2048,2]{1,0:T(8,128)S(1)} %copy.49, f32[]{:T(128)} %constant.10.clone.1), kind=kCustom, calls=%fused_computation.18 | custom fusion | flops 4096 | bytes 131584 | tf_op jit(solution)/shard_map/scatter-add | solution.py:124
  260.6 16.9 %scatter_fusion.1 = f32[2,16384]{0,1:T(8,128)} fusion(f32[2,16384]{0,1:T(8,128)} %scatter_custom_fusion.3, s32[2048]{0:T(1024)S(1)} %bitcast.377, f32[2048,2]{1,0:T(8,128)S(1)} %copy.50), kind=kCustom, calls=%fused_computation.10 | custom fusion | flops 4096 | bytes 57344 | tf_op jit(solution)/shard_map/scatter-add | solution.py:124
  277.5 12.2 %slice_reduce_fusion.1 = (f32[16384]{0:T(1024)S(1)}, f32[16384]{0:T(1024)S(1)}) fusion(f32[2,16384]{0,1:T(8,128)} %scatter_fusion.1), kind=kLoop, calls=%fused_computation.13 | loop fusion | bytes 262144 | tf_op jit(solution)/shard_map/slice | solution.py:138
  289.8 0.6 multiply_reduce_fusion.2
  290.5 41.0 %all-reduce.1 = (f32[]{:T(128)}, f32[]{:T(128)}) all-reduce(f32[]{:T(128)} %get-tuple-element.11, f32[]{:T(128)} %get-tuple-element.10), channel_id=1, replica_groups=mesh['cells'=8,'slab'=4] {'cells','slab'}, use_global_device_ids=true, to_apply=%region_14.15 | all-reduce | flops 2 | bytes 16 | tf_op jit(solution)/shard_map/psum | solution.py:142
  332.8 0.6 multiply_reduce_fusion.1
  333.5 42.0 %all-reduce = (f32[]{:T(128)}, f32[]{:T(128)}, f32[]{:T(128)}, f32[]{:T(128)}) all-reduce(f32[]{:T(128)} %get-tuple-element.9, f32[]{:T(128)} %get-tuple-element.8, f32[]{:T(128)} %get-tuple-element.7, f32[]{:T(128)} %get-tuple-element.6), channel_id=1, replica_groups=mesh['cells'=8,'slab'=4] {'cells','slab'}, use_global_device_ids=true, to_apply=%region_24.25 | all-reduce | flops 4 | bytes 32 | tf_op jit(solution)/shard_map/psum | solution.py:30
  378.3 0.6 pad_maximum_fusion.16
  378.8 0.7 pad_maximum_fusion
  (105 shorter events, 4.0 us)
Async XLA Ops:
  1.7 27.2 %collective-permute-start = (f32[16]{0:T(128)S(1)}, f32[16]{0:T(128)S(1)}, u32[]{:S(2)}, u32[]{:S(2)}) collective-permute-start(f32[16]{0:T(128)S(1)} %slice_reduce_fusion.4), channel_id=1, source_target_pairs={{0,4},{4,8},{8,12},{12,16},{16,20},{20,24},{24,28},{1,5},{5,9},{9,... | collective-permute-start | bytes 200 | tf_op jit(solution)/shard_map/ppermute | solution.py:13
  7.5 81.4 %copy-start.2 = (f32[16,1024]{1,0:T(8,128)}, f32[16,1024]{1,0:T(8,128)S(1)}, u32[]{:S(2)}) copy-start(f32[16,1024]{1,0:T(8,128)S(1)} %broadcast_select_fusion) | copy-start | bytes 196612
  7.5 21.4 %collective-permute-start.1 = (f32[1024]{0:T(1024)S(1)}, f32[1024]{0:T(1024)S(1)}, u32[]{:S(2)}, u32[]{:S(2)}) collective-permute-start(f32[1024]{0:T(1024)S(1)} %bitcast.389), channel_id=1, source_target_pairs={{0,1},{1,2},{2,3},{4,5},{5,6},{6,7},{8,9},{9,10},{10,11},{12,13},{... | collective-permute-start | bytes 12296 | tf_op jit(solution)/shard_map/ppermute | solution.py:13
  10.3 94.4 %collective-permute-start.7 = (f32[2048]{0:T(1024)S(1)}, f32[2048]{0:T(1024)S(1)}, u32[]{:S(2)}, u32[]{:S(2)}) collective-permute-start(f32[2048]{0:T(1024)S(1)} %fusion.81), channel_id=1, source_target_pairs={{0,4},{4,8},{8,12},{12,16},{16,20},{20,24},{24,28},{1,5},{5,9},{9,... | collective-permute-start | bytes 24584 | tf_op jit(solution)/shard_map/ppermute | solution.py:13
  15.5 28.7 %copy-start.11 = (s32[2048]{0:T(1024)}, s32[2048]{0:T(1024)S(1)}, u32[]{:S(2)}) copy-start(s32[2048]{0:T(1024)S(1)} %broadcast_clamp_fusion) | copy-start | bytes 24580
  16.2 73.4 %copy-start.15 = (s32[2048,1]{0,1:T(1,128)}, s32[2048,1]{0,1:T(1,128)S(1)}, u32[]{:S(2)}) copy-start(s32[2048,1]{0,1:T(1,128)S(1)} %compare_select_fusion.1) | copy-start | bytes 24580
  16.2 38.5 %copy-start.12 = (s32[2048]{0:T(1024)}, s32[2048]{0:T(1024)S(1)}, u32[]{:S(2)}) copy-start(s32[2048]{0:T(1024)S(1)} %broadcast_clamp_fusion.1) | copy-start | bytes 24580
  17.6 69.9 %copy-start.17 = (s32[128]{0:T(128)}, s32[128]{0:T(128)S(1)}, u32[]{:S(2)}) copy-start(s32[128]{0:T(128)S(1)} %fusion.83) | copy-start | bytes 1540
  19.5 55.3 %copy-start.16 = (s32[1024]{0:T(1024)}, s32[1024]{0:T(1024)S(1)}, u32[]{:S(2)}) copy-start(s32[1024]{0:T(1024)S(1)} %pad_clamp_fusion) | copy-start | bytes 12292
  19.5 9.4 %copy-start = (f32[2,4,16,1024]{3,2,1,0:T(8,128)S(1)}, f32[2,4,16,1024]{3,2,1,0:T(8,128)}, u32[]{:S(2)}) copy-start(f32[2,4,16,1024]{3,2,1,0:T(8,128)} %param.14) | copy-start | bytes 1572868
  19.5 9.4 %copy-start.1 = (f32[2,2,16,1024]{3,2,1,0:T(8,128)S(1)}, f32[2,2,16,1024]{3,2,1,0:T(8,128)}, u32[]{:S(2)}) copy-start(f32[2,2,16,1024]{3,2,1,0:T(8,128)} %param.15) | copy-start | bytes 786436
  19.5 9.4 %copy-start.9 = (f32[16,1024]{1,0:T(8,128)S(1)}, f32[16,1024]{1,0:T(8,128)}, u32[]{:S(2)}) copy-start(f32[16,1024]{1,0:T(8,128)} %param.17) | copy-start | bytes 196612
  19.5 9.4 %copy-start.10 = (f32[16,1024]{1,0:T(8,128)S(1)}, f32[16,1024]{1,0:T(8,128)}, u32[]{:S(2)}) copy-start(f32[16,1024]{1,0:T(8,128)} %param.18) | copy-start | bytes 196612
  29.1 59.8 %copy-start.3 = (f32[16,1024]{1,0:T(8,128)}, f32[16,1024]{1,0:T(8,128)S(1)}, u32[]{:S(2)}) copy-start(f32[16,1024]{1,0:T(8,128)S(1)} %get-tuple-element.26) | copy-start | bytes 196612
  29.1 59.8 %copy-start.4 = (f32[16,1024]{1,0:T(8,128)}, f32[16,1024]{1,0:T(8,128)S(1)}, u32[]{:S(2)}) copy-start(f32[16,1024]{1,0:T(8,128)S(1)} %get-tuple-element.27) | copy-start | bytes 196612
  34.4 41.6 %copy-start.18 = (s32[1,128]{1,0:T(1,128)S(1)}, s32[1,128]{1,0:T(1,128)}, u32[]{:S(2)}) copy-start(s32[1,128]{1,0:T(1,128)} %param.24) | copy-start | bytes 1540
  34.4 41.6 %copy-start.19 = (f32[1,128]{1,0:T(1,128)S(1)}, f32[1,128]{1,0:T(1,128)}, u32[]{:S(2)}) copy-start(f32[1,128]{1,0:T(1,128)} %param.25) | copy-start | bytes 1540
  53.4 35.8 %collective-permute-start.6 = (f32[2,2048]{1,0:T(2,128)S(1)}, f32[2,2048]{1,0:T(2,128)S(1)}, u32[]{:S(2)}, u32[]{:S(2)}) collective-permute-start(f32[2,2048]{1,0:T(2,128)S(1)} %bitcast.380), channel_id=1, source_target_pairs={{4,0},{8,4},{12,8},{16,12},{20,16},{24,20},{28,24},{5,1},{9,5},{13... | collective-permute-start | bytes 49160 | tf_op jit(solution)/shard_map/ppermute | solution.py:13
  63.9 40.9 %collective-permute-start.8 = (f32[2,2048]{1,0:T(2,128)S(1)}, f32[2,2048]{1,0:T(2,128)S(1)}, u32[]{:S(2)}, u32[]{:S(2)}) collective-permute-start(f32[2,2048]{1,0:T(2,128)S(1)} %bitcast.381), channel_id=1, source_target_pairs={{0,4},{4,8},{8,12},{12,16},{16,20},{20,24},{24,28},{1,5},{5,9},{9,... | collective-permute-start | bytes 49160 | tf_op jit(solution)/shard_map/ppermute | solution.py:13
  68.5 14.3 %collective-permute-start.2 = (f32[2,16,1]{2,1,0:T(8,128)S(1)}, f32[2,16,1]{2,1,0:T(8,128)S(1)}, u32[]{:S(2)}, u32[]{:S(2)}) collective-permute-start(f32[2,16,1]{2,1,0:T(8,128)S(1)} %get-tuple-element.42), channel_id=1, source_target_pairs={{4,0},{8,4},{12,8},{16,12},{20,16},{24,20},{28,24},{5,1},{9,5},{13... | collective-permute-start | bytes 392 | tf_op jit(solution)/shard_map/ppermute | solution.py:24
  69.8 13.0 %collective-permute-start.3 = (f32[2,16,1]{2,1,0:T(8,128)S(1)}, f32[2,16,1]{2,1,0:T(8,128)S(1)}, u32[]{:S(2)}, u32[]{:S(2)}) collective-permute-start(f32[2,16,1]{2,1,0:T(8,128)S(1)} %get-tuple-element.43), channel_id=1, source_target_pairs={{0,4},{4,8},{8,12},{12,16},{16,20},{20,24},{24,28},{1,5},{5,9},{9,... | collective-permute-start | bytes 392 | tf_op jit(solution)/shard_map/ppermute | solution.py:21
  82.8 4.5 %copy-start.20 = (f32[16]{0:T(128)}, f32[16]{0:T(128)S(1)}, u32[]{:S(2)}) copy-start(f32[16]{0:T(128)S(1)} %get-tuple-element.23) | copy-start | bytes 196
  82.9 5.9 %collective-permute-start.4 = (f32[2,1,1026]{2,1,0:T(1,128)S(1)}, f32[2,1,1026]{2,1,0:T(1,128)S(1)}, u32[]{:S(2)}, u32[]{:S(2)}) collective-permute-start(f32[2,1,1026]{2,1,0:T(1,128)S(1)} %get-tuple-element.38), channel_id=1, source_target_pairs={{1,0},{2,1},{3,2},{5,4},{6,5},{7,6},{9,8},{10,9},{11,10},{13,12},{... | collective-permute-start | bytes 24632 | tf_op jit(solution)/shard_map/ppermute | solution.py:24
  84.2 4.6 %collective-permute-start.5 = (f32[2,1,1026]{2,1,0:T(1,128)S(1)}, f32[2,1,1026]{2,1,0:T(1,128)S(1)}, u32[]{:S(2)}, u32[]{:S(2)}) collective-permute-start(f32[2,1,1026]{2,1,0:T(1,128)S(1)} %get-tuple-element.39), channel_id=1, source_target_pairs={{0,1},{1,2},{2,3},{4,5},{5,6},{6,7},{8,9},{9,10},{10,11},{12,13},{... | collective-permute-start | bytes 24632 | tf_op jit(solution)/shard_map/ppermute | solution.py:21
  104.7 29.8 %copy-start.14 = (f32[2048]{0:T(1024)}, f32[2048]{0:T(1024)S(1)}, u32[]{:S(2)}) copy-start(f32[2048]{0:T(1024)S(1)} %collective-permute-done.7) | copy-start | bytes 24580
  122.0 57.5 %copy-start.7 = (f32[2,2,16,1024]{3,2,1,0:T(8,128)S(1)}, f32[2,2,16,1024]{3,2,1,0:T(8,128)}, u32[]{:S(2)}) copy-start(f32[2,2,16,1024]{3,2,1,0:T(8,128)} %param.16) | copy-start | bytes 786436
  122.0 57.5 %copy-start.8 = (f32[2,2,16,1024]{3,2,1,0:T(8,128)S(1)}, f32[2,2,16,1024]{3,2,1,0:T(8,128)}, u32[]{:S(2)}) copy-start(f32[2,2,16,1024]{3,2,1,0:T(8,128)} %param.13) | copy-start | bytes 786436
  134.6 44.9 %copy-start.5 = (f32[1,16,1024]{2,1,0:T(8,128)}, f32[1,16,1024]{2,1,0:T(8,128)S(1)}, u32[]{:S(2)}) copy-start(f32[1,16,1024]{2,1,0:T(8,128)S(1)} %get-tuple-element.33) | copy-start | bytes 196612
  185.0 9.8 %copy-start.13 = (s32[2048]{0:T(1024)S(1)}, s32[2048]{0:T(1024)}, u32[]{:S(2)}) copy-start(s32[2048]{0:T(1024)} %copy-done.12) | copy-start | bytes 24580
  215.0 20.1 %collective-permute-start.10 = (f32[2,16,1]{2,1,0:T(8,128)S(1)}, f32[2,16,1]{2,1,0:T(8,128)S(1)}, u32[]{:S(2)}, u32[]{:S(2)}) collective-permute-start(f32[2,16,1]{2,1,0:T(8,128)S(1)} %get-tuple-element.41), channel_id=1, source_target_pairs={{0,4},{4,8},{8,12},{12,16},{16,20},{20,24},{24,28},{1,5},{5,9},{9,... | collective-permute-start | bytes 392 | tf_op jit(solution)/shard_map/ppermute | solution.py:21
  219.4 15.7 %collective-permute-start.9 = (f32[2,16,1]{2,1,0:T(8,128)S(1)}, f32[2,16,1]{2,1,0:T(8,128)S(1)}, u32[]{:S(2)}, u32[]{:S(2)}) collective-permute-start(f32[2,16,1]{2,1,0:T(8,128)S(1)} %get-tuple-element.40), channel_id=1, source_target_pairs={{4,0},{8,4},{12,8},{16,12},{20,16},{24,20},{28,24},{5,1},{9,5},{13... | collective-permute-start | bytes 392 | tf_op jit(solution)/shard_map/ppermute | solution.py:24
  221.0 22.8 %collective-permute-start.14 = (f32[2,2048]{1,0:T(2,128)S(1)}, f32[2,2048]{1,0:T(2,128)S(1)}, u32[]{:S(2)}, u32[]{:S(2)}) collective-permute-start(f32[2,2048]{1,0:T(2,128)S(1)} %bitcast.382), channel_id=1, source_target_pairs={{0,4},{4,8},{8,12},{12,16},{16,20},{20,24},{24,28},{1,5},{5,9},{9,... | collective-permute-start | bytes 49160 | tf_op jit(solution)/shard_map/ppermute | solution.py:13
  225.9 19.0 %collective-permute-start.13 = (f32[2,2048]{1,0:T(2,128)S(1)}, f32[2,2048]{1,0:T(2,128)S(1)}, u32[]{:S(2)}, u32[]{:S(2)}) collective-permute-start(f32[2,2048]{1,0:T(2,128)S(1)} %bitcast.383), channel_id=1, source_target_pairs={{4,0},{8,4},{12,8},{16,12},{20,16},{24,20},{28,24},{5,1},{9,5},{13... | collective-permute-start | bytes 49160 | tf_op jit(solution)/shard_map/ppermute | solution.py:13
  235.3 6.7 %collective-permute-start.11 = (f32[2,1,1026]{2,1,0:T(1,128)S(1)}, f32[2,1,1026]{2,1,0:T(1,128)S(1)}, u32[]{:S(2)}, u32[]{:S(2)}) collective-permute-start(f32[2,1,1026]{2,1,0:T(1,128)S(1)} %get-tuple-element.36), channel_id=1, source_target_pairs={{1,0},{2,1},{3,2},{5,4},{6,5},{7,6},{9,8},{10,9},{11,10},{13,12},{... | collective-permute-start | bytes 24632 | tf_op jit(solution)/shard_map/ppermute | solution.py:24
  236.6 5.4 %collective-permute-start.12 = (f32[2,1,1026]{2,1,0:T(1,128)S(1)}, f32[2,1,1026]{2,1,0:T(1,128)S(1)}, u32[]{:S(2)}, u32[]{:S(2)}) collective-permute-start(f32[2,1,1026]{2,1,0:T(1,128)S(1)} %get-tuple-element.37), channel_id=1, source_target_pairs={{0,1},{1,2},{2,3},{4,5},{5,6},{6,7},{8,9},{9,10},{10,11},{12,13},{... | collective-permute-start | bytes 24632 | tf_op jit(solution)/shard_map/ppermute | solution.py:21
  277.5 12.3 %copy-start.6 = (f32[2,16,1024]{2,1,0:T(8,128)S(1)}, f32[2,16,1024]{2,1,0:T(8,128)}, u32[]{:S(2)}) copy-start(f32[2,16,1024]{2,1,0:T(8,128)} %fusion.10) | copy-start | bytes 393220
where the time goes:
time: 381 us; the launch traced here: 380 us
  blocking collectives  138 us (36%)
  other arithmetic  101 us (27%)
  local copies, waits for them, and re-layouts  87.7 us (23%)
  starting transfers between devices  42 us (11%)
  between operations  7.48 us (2%)
    psum x2, blocking collectives, per_device(): lax.psum((jnp.sum(residual * image), jnp.sum(image * image)), ('cells', '...  83.9 us
    scatter-add x4, other arithmetic, per_device(): jnp.zeros_like(flat).at[:, near_cells].add(flux_right).at[:, far_cells]  64.3 us
    psum x1, blocking collectives, squares(): return lax.psum(jnp.sum(residual * residual), ('cells', 'slab'))  42 us
    slice x2, local copies, waits for them, and re-layouts, per_device(): fault_term[0]  24.7 us
    ppermute x7, starting transfers between devices, shifted(): return lax.ppermute(value, axis, pairs)  21.4 us
    mul x4, other arithmetic, per_device(): scaled = mobile * precond  19.6 us
    gather x4, local copies, waits for them, and re-layouts, per_device(): picks_far = flat[:, far_cells]  19.3 us
    gather x4, local copies, waits for them, and re-layouts, per_device(): picks_near = flat[:, near_cells]  18.3 us
  transfers between devices with their start and end apart: 15, of which 0 were waited for; matrix products, arithmetic and copies ran while one was open for 20% of the time, Pallas kernels for 0%

commit v1 on v0

--- a/solution.py
+++ b/solution.py
@@ -140,7 +140,7 @@
         second = block[2] * precond[0] + block[3] * precond[1] + laplace[1] + fault_term[1]
         image = jnp.stack([first, second])
         along, energy = lax.psum(
-            (jnp.sum(residual * image), jnp.sum(image * image)), ("cells", "slab")
+            lax.psum((jnp.sum(residual * image), jnp.sum(image * image)), "slab"), "cells"
         )
         history.append(jnp.sqrt(norm_square))
         alpha = along / energy

time: 381 us -> 347 us (0.911)
  blocking collectives: 138 us -> 107 us
    psum x2 -> x4, blocking collectives: 83.9 us -> 57.1 us  [the longest x2 41.6 us: per_device(): lax.psum(lax.psum((jnp.sum(residual * image), jnp.sum(image * image)), 's...]
    psum x1, blocking collectives: 42 us -> 37.3 us  [squares(): return lax.psum(jnp.sum(residual * residual), ('cells', 'slab'))]
  transfers between devices with their start and end apart: 15 -> 15, of which waited for: 0 -> 0; matrix products, arithmetic and copies ran while one was open for 20% -> 22% of each run, Pallas kernels for 0% -> 0%
where the time goes in v1:
time: 347 us; the launch traced here: 345 us
  blocking collectives  107 us (31%)
  other arithmetic  101 us (29%)
  local copies, waits for them, and re-layouts  87.7 us (25%)
  starting transfers between devices  38.9 us (11%)
  between operations  7.48 us (2%)
    scatter-add x4, other arithmetic, per_device(): jnp.zeros_like(flat).at[:, near_cells].add(flux_right).at[:, far_cells]  64.3 us
    psum x2, blocking collectives, per_device(): lax.psum(lax.psum((jnp.sum(residual * image), jnp.sum(image * image)), 's...  41.6 us
    psum x1, blocking collectives, squares(): return lax.psum(jnp.sum(residual * residual), ('cells', 'slab'))  37.3 us
    slice x2, local copies, waits for them, and re-layouts, per_device(): fault_term[0]  24.7 us
    ppermute x7, starting transfers between devices, shifted(): return lax.ppermute(value, axis, pairs)  21.4 us
    mul x4, other arithmetic, per_device(): scaled = mobile * precond  19.6 us
    gather x4, local copies, waits for them, and re-layouts, per_device(): picks_far = flat[:, far_cells]  19.3 us
    gather x4, local copies, waits for them, and re-layouts, per_device(): picks_near = flat[:, near_cells]  18.3 us
  transfers between devices with their start and end apart: 15, of which 0 were waited for; matrix products, arithmetic and copies ran while one was open for 22% of the time, Pallas kernels for 0%

profile of v1, /device:TPU:0, one launch (start us, length us, event | category | flops | bytes accessed | tf_op | source)
XLA Modules:
  0.0 344.9 jit_solution(14053276001658575606)
XLA Ops:
  0.6 0.9 broadcast_select_fusion.1
  1.7 4.9 %collective-permute-start = (f32[16]{0:T(128)S(1)}, f32[16]{0:T(128)S(1)}, u32[]{:S(2)}, u32[]{:S(2)}) collective-permute-start(f32[16]{0:T(128)S(1)} %slice_reduce_fusion.4), channel_id=1, source_target_pairs={{0,4},{4,8},{8,12},{12,16},{16,20},{20,24},{24,28},{1,5},{5,9},{9,... | collective-permute-start | bytes 200 | tf_op jit(solution)/shard_map/ppermute | solution.py:13
  6.6 0.9 broadcast_select_fusion
  7.5 1.5 collective-permute-start.1
  9.6 0.7 fusion.81
  10.3 3.4 collective-permute-start.7
  13.8 1.0 fusion.91
  14.7 0.7 compare_select_fusion
  15.5 0.7 compare_select_fusion.1
  16.2 0.7 and_select_fusion
  16.9 0.7 fusion.83
  17.6 1.0 multiply_add_fusion
  18.6 0.9 convolution_bitcast_fusion.3
  19.6 4.6 %copy.39 = f32[1,2,16,1024]{1,3,2,0:T(8,128)} copy(f32[1,2,16,1024]{3,2,1,0:T(8,128)S(1)} %get-tuple-element.39) | data formatting | bytes 262144 | tf_op jit(solution)/shard_map/slice | solution.py:87
  24.2 4.7 %copy.45 = f32[1,2,16,1024]{1,3,2,0:T(8,128)} copy(f32[1,2,16,1024]{3,2,1,0:T(8,128)S(1)} %get-tuple-element.38) | data formatting | bytes 262144 | tf_op jit(solution)/shard_map/slice | solution.py:87
  29.4 5.0 %copy.40 = f32[2,16384]{0,1:T(8,128)} copy(f32[2,16384]{1,0:T(2,128)S(1)} %pad_maximum_fusion.10) | data formatting | bytes 262144 | tf_op jit(solution)/shard_map/stack | solution.py:98
  34.4 9.8 %bitcast_multiply_fusion.1 = f32[2,16384]{0,1:T(8,128)} fusion(f32[2,16384]{0,1:T(8,128)} %copy.40, f32[1,2,16,1024]{1,3,2,0:T(8,128)} %copy.39), kind=kLoop, calls=%fused_computation.17 | loop fusion | flops 32768 | bytes 393216 | tf_op jit(solution)/shard_map/mul | solution.py:104
  44.2 8.8 %gather_fusion.1 = f32[2048,2]{1,0:T(8,128)S(1)} fusion(f32[2,16384]{0,1:T(8,128)} %bitcast_multiply_fusion.1, s32[2048]{0:T(1024)S(1)} %broadcast_clamp_fusion), kind=kCustom, calls=%fused_computation.1 | custom fusion | bytes 40960 | tf_op jit(solution)/shard_map/gather | solution.py:107
  53.4 1.3 collective-permute-start.6
  54.7 8.8 %gather_fusion = f32[2048,2]{1,0:T(8,128)S(1)} fusion(f32[2,16384]{0,1:T(8,128)} %bitcast_multiply_fusion.1, s32[2048]{0:T(1024)S(1)} %broadcast_clamp_fusion.1), kind=kCustom, calls=%fused_computation | custom fusion | bytes 40960 | tf_op jit(solution)/shard_map/gather | solution.py:106
  63.9 4.5 %collective-permute-start.8 = (f32[2,2048]{1,0:T(2,128)S(1)}, f32[2,2048]{1,0:T(2,128)S(1)}, u32[]{:S(2)}, u32[]{:S(2)}) collective-permute-start(f32[2,2048]{1,0:T(2,128)S(1)} %bitcast.381), channel_id=1, source_target_pairs={{0,4},{4,8},{8,12},{12,16},{16,20},{20,24},{24,28},{1,5},{5,9},{9,... | collective-permute-start | bytes 49160 | tf_op jit(solution)/shard_map/ppermute | solution.py:13
  68.5 1.3 collective-permute-start.2
  69.8 5.0 %collective-permute-start.3 = (f32[2,16,1]{2,1,0:T(8,128)S(1)}, f32[2,16,1]{2,1,0:T(8,128)S(1)}, u32[]{:S(2)}, u32[]{:S(2)}) collective-permute-start(f32[2,16,1]{2,1,0:T(8,128)S(1)} %get-tuple-element.47), channel_id=1, source_target_pairs={{0,4},{4,8},{8,12},{12,16},{16,20},{20,24},{24,28},{1,5},{5,9},{9,... | collective-permute-start | bytes 392 | tf_op jit(solution)/shard_map/ppermute | solution.py:21
  74.8 1.1 gather_fusion.2
  76.2 6.6 %all-reduce.5 = (f32[16]{0:T(128)S(1)}, f32[16]{0:T(128)S(1)}) all-reduce(f32[16]{0:T(128)S(1)} %convolution_bitcast_fusion.4, f32[16]{0:T(128)S(1)} %convolution_bitcast_fusion.3), channel_id=1, replica_groups=mesh['cells'=8,'slab'=4] {'slab'}, use_global_device_ids=true, to_apply=%region_2.3 | all-reduce | flops 32 | bytes 256 | tf_op jit(solution)/shard_map/psum | solution.py:129
  82.9 1.3 collective-permute-start.4
  84.2 3.0 collective-permute-start.5
  87.5 1.3 scatter_custom_fusion.2
  89.2 0.4 copy.43
  89.6 15.2 %scatter_custom_fusion = f32[2,16384]{0,1:T(8,128)} fusion(s32[2048]{0:T(1024)S(1)} %bitcast.386, f32[2048,2]{1,0:T(8,128)S(1)} %copy.43, f32[]{:T(128)} %constant.10.clone.1), kind=kCustom, calls=%fused_computation.20 | custom fusion | flops 4096 | bytes 131076 | tf_op jit(solution)/shard_map/scatter-add | solution.py:124
  104.8 0.4 copy.44
  105.1 16.9 %scatter_fusion = f32[2,16384]{0,1:T(8,128)} fusion(f32[2,16384]{0,1:T(8,128)} %scatter_custom_fusion, s32[2048]{0:T(1024)S(1)} %bitcast.376, f32[2048,2]{1,0:T(8,128)S(1)} %copy.44), kind=kCustom, calls=%fused_computation.7 | custom fusion | flops 4096 | bytes 57344 | tf_op jit(solution)/shard_map/scatter-add | solution.py:124
  122.0 12.5 %slice_reduce_fusion.3 = (f32[16384]{0:T(1024)S(1)}, f32[16384]{0:T(1024)S(1)}) fusion(f32[2,16384]{0,1:T(8,128)} %scatter_fusion), kind=kLoop, calls=%fused_computation.15 | loop fusion | bytes 262144 | tf_op jit(solution)/shard_map/slice | solution.py:138
  134.7 0.7 multiply_reduce_fusion.4
  135.3 7.5 %all-reduce.4 = (f32[]{:T(128)}, f32[]{:T(128)}) all-reduce(f32[]{:T(128)} %get-tuple-element.13, f32[]{:T(128)} %get-tuple-element.12), channel_id=1, replica_groups=mesh['cells'=8,'slab'=4] {'slab'}, use_global_device_ids=true, to_apply=%region_6.7 | all-reduce | flops 2 | bytes 16 | tf_op jit(solution)/shard_map/psum | solution.py:143
  142.9 20.6 %all-reduce.2 = (f32[]{:T(128)}, f32[]{:T(128)}) all-reduce(f32[]{:T(128)} %get-tuple-element.24, f32[]{:T(128)} %get-tuple-element.25), channel_id=1, replica_groups=mesh['cells'=8,'slab'=4] {'cells'}, use_global_device_ids=true, to_apply=%region_7.8 | all-reduce | flops 2 | bytes 16 | tf_op jit(solution)/shard_map/psum | solution.py:142
  165.2 5.0 %copy.46 = f32[2,16384]{0,1:T(8,128)} copy(f32[2,16384]{1,0:T(2,128)S(1)} %pad_maximum_fusion.12) | data formatting | bytes 262144 | tf_op jit(solution)/shard_map/stack | solution.py:98
  170.2 9.8 %bitcast_multiply_fusion = f32[2,16384]{0,1:T(8,128)} fusion(f32[2,16384]{0,1:T(8,128)} %copy.46, f32[1,2,16,1024]{1,3,2,0:T(8,128)} %copy.45), kind=kLoop, calls=%fused_computation.16 | loop fusion | flops 32768 | bytes 393216 | tf_op jit(solution)/shard_map/mul | solution.py:104
  180.0 8.8 %gather_fusion.3 = f32[2048,2]{1,0:T(8,128)S(1)} fusion(f32[2,16384]{0,1:T(8,128)} %bitcast_multiply_fusion, s32[2048]{0:T(1024)S(1)} %copy-done.13), kind=kCustom, calls=%fused_computation.3 | custom fusion | bytes 40960 | tf_op jit(solution)/shard_map/gather | solution.py:106
  188.9 9.8 %gather_fusion.4 = f32[2048,2]{1,0:T(8,128)S(1)} fusion(f32[2,16384]{0,1:T(8,128)} %bitcast_multiply_fusion, s32[2048]{0:T(1024)} %copy-done.11), kind=kCustom, calls=%fused_computation.4 | custom fusion | bytes 40960 | tf_op jit(solution)/shard_map/gather | solution.py:107
  198.7 1.5 fusion.31
  200.3 1.3 collective-permute-start.10
  201.6 1.3 collective-permute-start.9
  203.2 4.5 %collective-permute-start.14 = (f32[2,2048]{1,0:T(2,128)S(1)}, f32[2,2048]{1,0:T(2,128)S(1)}, u32[]{:S(2)}, u32[]{:S(2)}) collective-permute-start(f32[2,2048]{1,0:T(2,128)S(1)} %bitcast.382), channel_id=1, source_target_pairs={{0,4},{4,8},{8,12},{12,16},{16,20},{20,24},{24,28},{1,5},{5,9},{9,... | collective-permute-start | bytes 49160 | tf_op jit(solution)/shard_map/ppermute | solution.py:13
  208.1 1.3 collective-permute-start.13
  209.4 1.3 gather_fusion.5
  210.7 0.9 convolution_bitcast_fusion.1
  211.5 5.7 %psum.111 = f32[16]{0:T(128)S(1)} all-reduce(f32[16]{0:T(128)S(1)} %convolution_bitcast_fusion.1), channel_id=1, replica_groups=mesh['cells'=8,'slab'=4] {'slab'}, use_global_device_ids=true, to_apply=%region_13.14 | all-reduce | flops 16 | bytes 128 | tf_op jit(solution)/shard_map/psum | solution.py:129
  217.4 1.3 collective-permute-start.11
  218.7 3.0 collective-permute-start.12
  221.7 0.9 fusion.7
  222.6 1.5 scatter_custom_fusion.5
  224.1 1.8 fusion.10
  225.9 0.7 negate_bitcast_fusion
  227.4 15.3 %scatter_custom_fusion.3 = f32[2,16384]{0,1:T(8,128)} fusion(s32[2048]{0:T(1024)} %bitcast.387, f32[2048,2]{1,0:T(8,128)S(1)} %copy.49, f32[]{:T(128)} %constant.10.clone.1), kind=kCustom, calls=%fused_computation.18 | custom fusion | flops 4096 | bytes 131584 | tf_op jit(solution)/shard_map/scatter-add | solution.py:124
  242.7 16.9 %scatter_fusion.1 = f32[2,16384]{0,1:T(8,128)} fusion(f32[2,16384]{0,1:T(8,128)} %scatter_custom_fusion.3, s32[2048]{0:T(1024)S(1)} %bitcast.377, f32[2048,2]{1,0:T(8,128)S(1)} %copy.50), kind=kCustom, calls=%fused_computation.10 | custom fusion | flops 4096 | bytes 57344 | tf_op jit(solution)/shard_map/scatter-add | solution.py:124
  259.6 12.2 %slice_reduce_fusion.1 = (f32[16384]{0:T(1024)S(1)}, f32[16384]{0:T(1024)S(1)}) fusion(f32[2,16384]{0,1:T(8,128)} %scatter_fusion.1), kind=kLoop, calls=%fused_computation.13 | loop fusion | bytes 262144 | tf_op jit(solution)/shard_map/slice | solution.py:138
  271.9 0.6 multiply_reduce_fusion.2
  272.6 7.9 %all-reduce.3 = (f32[]{:T(128)}, f32[]{:T(128)}) all-reduce(f32[]{:T(128)} %get-tuple-element.11, f32[]{:T(128)} %get-tuple-element.10), channel_id=1, replica_groups=mesh['cells'=8,'slab'=4] {'slab'}, use_global_device_ids=true, to_apply=%region_16.17 | all-reduce | flops 2 | bytes 16 | tf_op jit(solution)/shard_map/psum | solution.py:143
  280.5 21.0 %all-reduce.1 = (f32[]{:T(128)}, f32[]{:T(128)}) all-reduce(f32[]{:T(128)} %get-tuple-element.22, f32[]{:T(128)} %get-tuple-element.23), channel_id=1, replica_groups=mesh['cells'=8,'slab'=4] {'cells'}, use_global_device_ids=true, to_apply=%region_17.18 | all-reduce | flops 2 | bytes 16 | tf_op jit(solution)/shard_map/psum | solution.py:142
  302.8 0.6 multiply_reduce_fusion.1
  303.5 37.3 %all-reduce = (f32[]{:T(128)}, f32[]{:T(128)}, f32[]{:T(128)}, f32[]{:T(128)}) all-reduce(f32[]{:T(128)} %get-tuple-element.9, f32[]{:T(128)} %get-tuple-element.8, f32[]{:T(128)} %get-tuple-element.7, f32[]{:T(128)} %get-tuple-element.6), channel_id=1, replica_groups=mesh['cells'=8,'slab'=4] {'cells','slab'}, use_global_device_ids=true, to_apply=%region_28.29 | all-reduce | flops 4 | bytes 32 | tf_op jit(solution)/shard_map/psum | solution.py:30
  343.6 0.6 pad_maximum_fusion.16
  344.2 0.7 pad_maximum_fusion
  (107 shorter events, 4.7 us)
Async XLA Ops:
  1.7 27.2 %collective-permute-start = (f32[16]{0:T(128)S(1)}, f32[16]{0:T(128)S(1)}, u32[]{:S(2)}, u32[]{:S(2)}) collective-permute-start(f32[16]{0:T(128)S(1)} %slice_reduce_fusion.4), channel_id=1, source_target_pairs={{0,4},{4,8},{8,12},{12,16},{16,20},{20,24},{24,28},{1,5},{5,9},{9,... | collective-permute-start | bytes 200 | tf_op jit(solution)/shard_map/ppermute | solution.py:13
  7.5 81.4 %copy-start.2 = (f32[16,1024]{1,0:T(8,128)}, f32[16,1024]{1,0:T(8,128)S(1)}, u32[]{:S(2)}) copy-start(f32[16,1024]{1,0:T(8,128)S(1)} %broadcast_select_fusion) | copy-start | bytes 196612
  7.5 21.4 %collective-permute-start.1 = (f32[1024]{0:T(1024)S(1)}, f32[1024]{0:T(1024)S(1)}, u32[]{:S(2)}, u32[]{:S(2)}) collective-permute-start(f32[1024]{0:T(1024)S(1)} %bitcast.389), channel_id=1, source_target_pairs={{0,1},{1,2},{2,3},{4,5},{5,6},{6,7},{8,9},{9,10},{10,11},{12,13},{... | collective-permute-start | bytes 12296 | tf_op jit(solution)/shard_map/ppermute | solution.py:13
  10.3 94.4 %collective-permute-start.7 = (f32[2048]{0:T(1024)S(1)}, f32[2048]{0:T(1024)S(1)}, u32[]{:S(2)}, u32[]{:S(2)}) collective-permute-start(f32[2048]{0:T(1024)S(1)} %fusion.81), channel_id=1, source_target_pairs={{0,4},{4,8},{8,12},{12,16},{16,20},{20,24},{24,28},{1,5},{5,9},{9,... | collective-permute-start | bytes 24584 | tf_op jit(solution)/shard_map/ppermute | solution.py:13
  15.5 28.7 %copy-start.11 = (s32[2048]{0:T(1024)}, s32[2048]{0:T(1024)S(1)}, u32[]{:S(2)}) copy-start(s32[2048]{0:T(1024)S(1)} %broadcast_clamp_fusion) | copy-start | bytes 24580
  16.2 73.4 %copy-start.15 = (s32[2048,1]{0,1:T(1,128)}, s32[2048,1]{0,1:T(1,128)S(1)}, u32[]{:S(2)}) copy-start(s32[2048,1]{0,1:T(1,128)S(1)} %compare_select_fusion.1) | copy-start | bytes 24580
  16.2 38.5 %copy-start.12 = (s32[2048]{0:T(1024)}, s32[2048]{0:T(1024)S(1)}, u32[]{:S(2)}) copy-start(s32[2048]{0:T(1024)S(1)} %broadcast_clamp_fusion.1) | copy-start | bytes 24580
  17.6 69.9 %copy-start.17 = (s32[128]{0:T(128)}, s32[128]{0:T(128)S(1)}, u32[]{:S(2)}) copy-start(s32[128]{0:T(128)S(1)} %fusion.83) | copy-start | bytes 1540
  19.5 55.3 %copy-start.16 = (s32[1024]{0:T(1024)}, s32[1024]{0:T(1024)S(1)}, u32[]{:S(2)}) copy-start(s32[1024]{0:T(1024)S(1)} %pad_clamp_fusion) | copy-start | bytes 12292
  19.5 9.4 %copy-start = (f32[2,4,16,1024]{3,2,1,0:T(8,128)S(1)}, f32[2,4,16,1024]{3,2,1,0:T(8,128)}, u32[]{:S(2)}) copy-start(f32[2,4,16,1024]{3,2,1,0:T(8,128)} %param.14) | copy-start | bytes 1572868
  19.5 9.4 %copy-start.1 = (f32[2,2,16,1024]{3,2,1,0:T(8,128)S(1)}, f32[2,2,16,1024]{3,2,1,0:T(8,128)}, u32[]{:S(2)}) copy-start(f32[2,2,16,1024]{3,2,1,0:T(8,128)} %param.15) | copy-start | bytes 786436
  19.5 9.4 %copy-start.9 = (f32[16,1024]{1,0:T(8,128)S(1)}, f32[16,1024]{1,0:T(8,128)}, u32[]{:S(2)}) copy-start(f32[16,1024]{1,0:T(8,128)} %param.17) | copy-start | bytes 196612
  19.5 9.4 %copy-start.10 = (f32[16,1024]{1,0:T(8,128)S(1)}, f32[16,1024]{1,0:T(8,128)}, u32[]{:S(2)}) copy-start(f32[16,1024]{1,0:T(8,128)} %param.18) | copy-start | bytes 196612
  29.1 59.8 %copy-start.3 = (f32[16,1024]{1,0:T(8,128)}, f32[16,1024]{1,0:T(8,128)S(1)}, u32[]{:S(2)}) copy-start(f32[16,1024]{1,0:T(8,128)S(1)} %get-tuple-element.30) | copy-start | bytes 196612
  29.1 59.8 %copy-start.4 = (f32[16,1024]{1,0:T(8,128)}, f32[16,1024]{1,0:T(8,128)S(1)}, u32[]{:S(2)}) copy-start(f32[16,1024]{1,0:T(8,128)S(1)} %get-tuple-element.31) | copy-start | bytes 196612
  34.4 41.6 %copy-start.18 = (s32[1,128]{1,0:T(1,128)S(1)}, s32[1,128]{1,0:T(1,128)}, u32[]{:S(2)}) copy-start(s32[1,128]{1,0:T(1,128)} %param.24) | copy-start | bytes 1540
  34.4 41.6 %copy-start.19 = (f32[1,128]{1,0:T(1,128)S(1)}, f32[1,128]{1,0:T(1,128)}, u32[]{:S(2)}) copy-start(f32[1,128]{1,0:T(1,128)} %param.25) | copy-start | bytes 1540
  53.4 35.8 %collective-permute-start.6 = (f32[2,2048]{1,0:T(2,128)S(1)}, f32[2,2048]{1,0:T(2,128)S(1)}, u32[]{:S(2)}, u32[]{:S(2)}) collective-permute-start(f32[2,2048]{1,0:T(2,128)S(1)} %bitcast.380), channel_id=1, source_target_pairs={{4,0},{8,4},{12,8},{16,12},{20,16},{24,20},{28,24},{5,1},{9,5},{13... | collective-permute-start | bytes 49160 | tf_op jit(solution)/shard_map/ppermute | solution.py:13
  63.9 40.9 %collective-permute-start.8 = (f32[2,2048]{1,0:T(2,128)S(1)}, f32[2,2048]{1,0:T(2,128)S(1)}, u32[]{:S(2)}, u32[]{:S(2)}) collective-permute-start(f32[2,2048]{1,0:T(2,128)S(1)} %bitcast.381), channel_id=1, source_target_pairs={{0,4},{4,8},{8,12},{12,16},{16,20},{20,24},{24,28},{1,5},{5,9},{9,... | collective-permute-start | bytes 49160 | tf_op jit(solution)/shard_map/ppermute | solution.py:13
  68.5 14.3 %collective-permute-start.2 = (f32[2,16,1]{2,1,0:T(8,128)S(1)}, f32[2,16,1]{2,1,0:T(8,128)S(1)}, u32[]{:S(2)}, u32[]{:S(2)}) collective-permute-start(f32[2,16,1]{2,1,0:T(8,128)S(1)} %get-tuple-element.46), channel_id=1, source_target_pairs={{4,0},{8,4},{12,8},{16,12},{20,16},{24,20},{28,24},{5,1},{9,5},{13... | collective-permute-start | bytes 392 | tf_op jit(solution)/shard_map/ppermute | solution.py:24
  69.8 13.0 %collective-permute-start.3 = (f32[2,16,1]{2,1,0:T(8,128)S(1)}, f32[2,16,1]{2,1,0:T(8,128)S(1)}, u32[]{:S(2)}, u32[]{:S(2)}) collective-permute-start(f32[2,16,1]{2,1,0:T(8,128)S(1)} %get-tuple-element.47), channel_id=1, source_target_pairs={{0,4},{4,8},{8,12},{12,16},{16,20},{20,24},{24,28},{1,5},{5,9},{9,... | collective-permute-start | bytes 392 | tf_op jit(solution)/shard_map/ppermute | solution.py:21
  82.8 4.5 %copy-start.20 = (f32[16]{0:T(128)}, f32[16]{0:T(128)S(1)}, u32[]{:S(2)}) copy-start(f32[16]{0:T(128)S(1)} %get-tuple-element.27) | copy-start | bytes 196
  82.9 5.9 %collective-permute-start.4 = (f32[2,1,1026]{2,1,0:T(1,128)S(1)}, f32[2,1,1026]{2,1,0:T(1,128)S(1)}, u32[]{:S(2)}, u32[]{:S(2)}) collective-permute-start(f32[2,1,1026]{2,1,0:T(1,128)S(1)} %get-tuple-element.42), channel_id=1, source_target_pairs={{1,0},{2,1},{3,2},{5,4},{6,5},{7,6},{9,8},{10,9},{11,10},{13,12},{... | collective-permute-start | bytes 24632 | tf_op jit(solution)/shard_map/ppermute | solution.py:24
  84.2 4.6 %collective-permute-start.5 = (f32[2,1,1026]{2,1,0:T(1,128)S(1)}, f32[2,1,1026]{2,1,0:T(1,128)S(1)}, u32[]{:S(2)}, u32[]{:S(2)}) collective-permute-start(f32[2,1,1026]{2,1,0:T(1,128)S(1)} %get-tuple-element.43), channel_id=1, source_target_pairs={{0,1},{1,2},{2,3},{4,5},{5,6},{6,7},{8,9},{9,10},{10,11},{12,13},{... | collective-permute-start | bytes 24632 | tf_op jit(solution)/shard_map/ppermute | solution.py:21
  104.7 29.8 %copy-start.14 = (f32[2048]{0:T(1024)}, f32[2048]{0:T(1024)S(1)}, u32[]{:S(2)}) copy-start(f32[2048]{0:T(1024)S(1)} %collective-permute-done.7) | copy-start | bytes 24580
  122.0 42.8 %copy-start.7 = (f32[2,2,16,1024]{3,2,1,0:T(8,128)S(1)}, f32[2,2,16,1024]{3,2,1,0:T(8,128)}, u32[]{:S(2)}) copy-start(f32[2,2,16,1024]{3,2,1,0:T(8,128)} %param.16) | copy-start | bytes 786436
  122.0 42.8 %copy-start.8 = (f32[2,2,16,1024]{3,2,1,0:T(8,128)S(1)}, f32[2,2,16,1024]{3,2,1,0:T(8,128)}, u32[]{:S(2)}) copy-start(f32[2,2,16,1024]{3,2,1,0:T(8,128)} %param.13) | copy-start | bytes 786436
  134.6 30.2 %copy-start.5 = (f32[1,16,1024]{2,1,0:T(8,128)}, f32[1,16,1024]{2,1,0:T(8,128)S(1)}, u32[]{:S(2)}) copy-start(f32[1,16,1024]{2,1,0:T(8,128)S(1)} %get-tuple-element.37) | copy-start | bytes 196612
  170.2 9.8 %copy-start.13 = (s32[2048]{0:T(1024)S(1)}, s32[2048]{0:T(1024)}, u32[]{:S(2)}) copy-start(s32[2048]{0:T(1024)} %copy-done.12) | copy-start | bytes 24580
  200.3 16.9 %collective-permute-start.10 = (f32[2,16,1]{2,1,0:T(8,128)S(1)}, f32[2,16,1]{2,1,0:T(8,128)S(1)}, u32[]{:S(2)}, u32[]{:S(2)}) collective-permute-start(f32[2,16,1]{2,1,0:T(8,128)S(1)} %get-tuple-element.45), channel_id=1, source_target_pairs={{0,4},{4,8},{8,12},{12,16},{16,20},{20,24},{24,28},{1,5},{5,9},{9,... | collective-permute-start | bytes 392 | tf_op jit(solution)/shard_map/ppermute | solution.py:21
  201.6 15.7 %collective-permute-start.9 = (f32[2,16,1]{2,1,0:T(8,128)S(1)}, f32[2,16,1]{2,1,0:T(8,128)S(1)}, u32[]{:S(2)}, u32[]{:S(2)}) collective-permute-start(f32[2,16,1]{2,1,0:T(8,128)S(1)} %get-tuple-element.44), channel_id=1, source_target_pairs={{4,0},{8,4},{12,8},{16,12},{20,16},{24,20},{28,24},{5,1},{9,5},{13... | collective-permute-start | bytes 392 | tf_op jit(solution)/shard_map/ppermute | solution.py:24
  203.2 22.7 %collective-permute-start.14 = (f32[2,2048]{1,0:T(2,128)S(1)}, f32[2,2048]{1,0:T(2,128)S(1)}, u32[]{:S(2)}, u32[]{:S(2)}) collective-permute-start(f32[2,2048]{1,0:T(2,128)S(1)} %bitcast.382), channel_id=1, source_target_pairs={{0,4},{4,8},{8,12},{12,16},{16,20},{20,24},{24,28},{1,5},{5,9},{9,... | collective-permute-start | bytes 49160 | tf_op jit(solution)/shard_map/ppermute | solution.py:13
  208.1 18.9 %collective-permute-start.13 = (f32[2,2048]{1,0:T(2,128)S(1)}, f32[2,2048]{1,0:T(2,128)S(1)}, u32[]{:S(2)}, u32[]{:S(2)}) collective-permute-start(f32[2,2048]{1,0:T(2,128)S(1)} %bitcast.383), channel_id=1, source_target_pairs={{4,0},{8,4},{12,8},{16,12},{20,16},{24,20},{28,24},{5,1},{9,5},{13... | collective-permute-start | bytes 49160 | tf_op jit(solution)/shard_map/ppermute | solution.py:13
  217.4 6.7 %collective-permute-start.11 = (f32[2,1,1026]{2,1,0:T(1,128)S(1)}, f32[2,1,1026]{2,1,0:T(1,128)S(1)}, u32[]{:S(2)}, u32[]{:S(2)}) collective-permute-start(f32[2,1,1026]{2,1,0:T(1,128)S(1)} %get-tuple-element.40), channel_id=1, source_target_pairs={{1,0},{2,1},{3,2},{5,4},{6,5},{7,6},{9,8},{10,9},{11,10},{13,12},{... | collective-permute-start | bytes 24632 | tf_op jit(solution)/shard_map/ppermute | solution.py:24
  218.7 5.4 %collective-permute-start.12 = (f32[2,1,1026]{2,1,0:T(1,128)S(1)}, f32[2,1,1026]{2,1,0:T(1,128)S(1)}, u32[]{:S(2)}, u32[]{:S(2)}) collective-permute-start(f32[2,1,1026]{2,1,0:T(1,128)S(1)} %get-tuple-element.41), channel_id=1, source_target_pairs={{0,1},{1,2},{2,3},{4,5},{5,6},{6,7},{8,9},{9,10},{10,11},{12,13},{... | collective-permute-start | bytes 24632 | tf_op jit(solution)/shard_map/ppermute | solution.py:21
  259.6 12.3 %copy-start.6 = (f32[2,16,1024]{2,1,0:T(8,128)S(1)}, f32[2,16,1024]{2,1,0:T(8,128)}, u32[]{:S(2)}) copy-start(f32[2,16,1024]{2,1,0:T(8,128)} %fusion.10) | copy-start | bytes 393220
